TPU v7x, 32 devices: a whole 2x2x4 slice. The times are simulated.
32 devices in a mesh: dp: 4 (over z), ctx: 8 (over y, x, core).
Axes of the slice: x: 2, y: 2, z: 4, core: 2. Of those that a mesh axis runs over, the one named last changes fastest.
Arguments:
- mixed: bfloat16 [4, 1024, 4096], P('dp', 'ctx'), may hold values from -6 to 6
- conv_weight: float32 [4, 4096], replicated, may hold values from -3 to 3
- log_decay: float32 [4, 1024, 16], P('dp', 'ctx'), may hold values from -1 to 0
- write_rate: float32 [4, 1024, 16], P('dp', 'ctx'), may hold values from 0.1 to 0.95
- segment_ids: int32 [4, 1024], P('dp', 'ctx'), may hold values from 0 to 3, never falling along the last dimension, each value on 1 to 512 neighbouring positions
- cotangent: bfloat16 [4, 1024, 2048], P('dp', 'ctx'), may hold values from -6 to 6
Outputs:
- core_out: bfloat16 [4, 1024, 2048], P('dp', 'ctx')
- grad_mixed: bfloat16 [4, 1024, 4096], P('dp', 'ctx')
- grad_decay: float32 [4, 1024, 16], P('dp', 'ctx')
- grad_rate: float32 [4, 1024, 16], P('dp', 'ctx')
- grad_conv: float32 [4, 4096], replicated
Inputs may be any that keep to these rules, and one draw needn't show every extreme that they name: `segment_ids`: per sequence, segment numbers never fall along the positions; every number of 0 to 3 occurs, each on at most 512 positions.
All inputs are finite; a program needn't handle non-finite values.
Results may differ from a plain program's by a relative error of at most 0.00105.
Values may be sent and summed in bfloat16 or wider, within the bound.
No kernel may reach another device: no remote copies, remote signals or barrier semaphores. Data moves between devices by JAX's collectives and lax.ppermute only.
A program may use at most 320 MiB of HBM per device.

v0:
```python
import math
import jax
import jax.numpy as jnp
from jax import lax
from jax.sharding import PartitionSpec as P

HK = 8
HV = 16
DK = 128
DV = 128
BLOCK = 64
HIGHEST = lax.Precision.HIGHEST


def from_behind(x, axis, by):
    size = lax.axis_size(axis)
    pairs = [(i, i + by) for i in range(size) if 0 <= i + by < size]
    return lax.ppermute(x, axis, pairs)


def prefix(value, axis, join, neutral, backward):
    count, mine = (lax.axis_size(axis), lax.axis_index(axis))
    pieces = jax.tree.map(lambda part: lax.all_gather(part, axis), value)
    if backward:
        pieces = jax.tree.map(lambda part: part[::-1], pieces)
        mine = count - 1 - mine
    total = jax.tree.map(
        lambda part, zero: jnp.full_like(part, 0) + jnp.asarray(zero, part.dtype), value, neutral
    )

    def hop(position, total):
        longer = join(total, jax.tree.map(lambda part: part[position], pieces))
        return jax.tree.map(lambda new, old: jnp.where(position < mine, new, old), longer, total)

    return lax.fori_loop(0, count - 1, hop, total)


def prepare(mix_ext, seg_ext, conv_weight):
    margin = conv_weight.shape[0] - 1
    positions = mix_ext.shape[0] - margin
    current = seg_ext[margin:]
    summed = jnp.zeros((positions, mix_ext.shape[1]), jnp.float32)
    for tap_index in range(margin + 1):
        same_doc = (seg_ext[tap_index : tap_index + positions] == current).astype(jnp.float32)
        summed = (
            summed
            + conv_weight[tap_index][None, :]
            * mix_ext[tap_index : tap_index + positions]
            * same_doc[:, None]
        )
    activated = jax.nn.silu(summed)
    split_at = HK * DK
    queries = activated[:, :split_at].reshape(positions, HK, DK)
    keyset = activated[:, split_at : 2 * split_at].reshape(positions, HK, DK)
    values = activated[:, 2 * split_at :].reshape(positions, HV, DV)
    queries = (
        queries
        / jnp.sqrt(jnp.sum(queries * queries, axis=-1, keepdims=True) + 1e-06)
        / math.sqrt(DK)
    )
    keyset = keyset / jnp.sqrt(jnp.sum(keyset * keyset, axis=-1, keepdims=True) + 1e-06)
    repeats = HV // HK
    return (jnp.repeat(queries, repeats, axis=1), jnp.repeat(keyset, repeats, axis=1), values)


def unit_lower_inverse(strict_part):
    positions = strict_part.shape[-1]
    identity_matrix = jnp.eye(positions, dtype=jnp.float32)[None]
    result = identity_matrix - strict_part
    power = strict_part
    reach = 2
    while reach < positions:
        power = jnp.einsum("hij,hjk->hik", power, power, precision=HIGHEST)
        result = jnp.einsum("hij,hjk->hik", result, identity_matrix + power, precision=HIGHEST)
        reach = reach * 2
    return result


def block_parts(queries, keyset, values, log_decay, write_rate, segments, seg_before):
    positions = queries.shape[0]
    cumulative = jnp.cumsum(log_decay, axis=0)
    keep_state = (segments == seg_before).astype(jnp.float32)
    entering = jnp.exp(cumulative) * keep_state[:, None]
    token_position = lax.iota(jnp.int32, positions)
    same_doc = segments[:, None] == segments[None, :]
    strict = same_doc & (token_position[:, None] > token_position[None, :])
    causal = same_doc & (token_position[:, None] >= token_position[None, :])
    spread = cumulative.T[:, :, None] - cumulative.T[:, None, :]
    strict_decay = jnp.where(strict[None], jnp.exp(jnp.where(strict[None], spread, 0.0)), 0.0)
    causal_decay = jnp.where(causal[None], jnp.exp(jnp.where(causal[None], spread, 0.0)), 0.0)
    key_inner = jnp.einsum("ihd,jhd->hij", keyset, keyset, precision=HIGHEST)
    inverse = unit_lower_inverse(write_rate.T[:, :, None] * key_inner * strict_decay)
    targets = jnp.concatenate(
        [keyset * (write_rate * entering)[:, :, None], values * write_rate[:, :, None]], axis=2
    )
    solved = jnp.einsum("hij,hjd->hid", inverse, targets.transpose(1, 0, 2), precision=HIGHEST)
    write_keys = solved[:, :, :DK]
    write_values = solved[:, :, DK:]
    scores = jnp.einsum("ihd,jhd->hij", queries, keyset, precision=HIGHEST) * causal_decay
    final_sum = cumulative[-1]
    tail_decay = (
        jnp.exp(final_sum[None, :] - cumulative)
        * (segments == segments[-1]).astype(jnp.float32)[:, None]
    )
    carried = jnp.exp(final_sum) * keep_state[-1]
    tail_keys = (keyset * tail_decay[:, :, None]).transpose(1, 0, 2)
    queried = (queries * entering[:, :, None]).transpose(1, 0, 2)
    return (write_keys, write_values, scores, tail_keys, queried, carried)


def block_map(block_data):
    write_keys, write_values, scores, tail_keys, queried, carried = block_data
    identity_matrix = jnp.eye(DK, dtype=jnp.float32)
    transform = carried[:, None, None] * identity_matrix[None] - jnp.einsum(
        "hcd,hce->hde", tail_keys, write_keys, precision=HIGHEST
    )
    shift_term = jnp.einsum("hcd,hce->hde", tail_keys, write_values, precision=HIGHEST)
    return (transform, shift_term)


def block_apply(block_data, state_in):
    write_keys, write_values, scores, tail_keys, queried, carried = block_data
    fresh_values = write_values - jnp.einsum(
        "hcd,hde->hce", write_keys, state_in, precision=HIGHEST
    )
    output = jnp.einsum("hcd,hde->hce", queried, state_in, precision=HIGHEST)
    output = output + jnp.einsum("hij,hje->hie", scores, fresh_values, precision=HIGHEST)
    state_next = carried[:, None, None] * state_in + jnp.einsum(
        "hcd,hce->hde", tail_keys, fresh_values, precision=HIGHEST
    )
    return (output, state_next)


def section_one(mix_ext, conv_weight, log_decay, write_rate, seg_ext):
    queries, keyset, values = prepare(mix_ext, seg_ext, conv_weight)
    margin = conv_weight.shape[0] - 1
    positions = log_decay.shape[0]
    blocks = positions // BLOCK
    segments = seg_ext[margin:]
    before = seg_ext[margin - 1 : margin - 1 + positions : BLOCK]

    def blocked(tensor):
        return tensor.reshape((blocks, BLOCK) + tensor.shape[1:])

    return jax.vmap(block_parts)(
        blocked(queries),
        blocked(keyset),
        blocked(values),
        blocked(log_decay),
        blocked(write_rate),
        blocked(segments),
        before,
    )


def section_two(parts, state_in):

    def step_block(state_now, block_data):
        output, state_next = block_apply(block_data, state_now)
        return (state_next, output)

    state_out, outputs = lax.scan(step_block, state_in, parts)
    blocks = outputs.shape[0]
    return (outputs.transpose(0, 2, 1, 3).reshape(blocks * BLOCK, HV * DV), state_out)


def summarize(parts):
    identity_matrix = jnp.eye(DK, dtype=jnp.float32)
    initial = (
        jnp.broadcast_to(identity_matrix, (HV, DK, DK)),
        jnp.zeros((HV, DK, DV), jnp.float32),
    )

    def fold_block(carried_map, block_data):
        transform, shift_term = block_map(block_data)
        merged = jnp.einsum("hij,hjk->hik", transform, carried_map[0], precision=HIGHEST)
        moved = (
            jnp.einsum("hij,hjk->hik", transform, carried_map[1], precision=HIGHEST) + shift_term
        )
        return ((merged, moved), None)

    result, unused = lax.scan(fold_block, initial, parts)
    return result


def compose(earlier_map, later_map):
    merged = jnp.einsum("shij,shjk->shik", later_map[0], earlier_map[0], precision=HIGHEST)
    moved = (
        jnp.einsum("shij,shjk->shik", later_map[0], earlier_map[1], precision=HIGHEST)
        + later_map[1]
    )
    return (merged, moved)


def local(mixed, conv_weight, log_decay, write_rate, segment_ids, cotangent):
    margin = conv_weight.shape[0] - 1
    shifted_rows, shifted_segs = from_behind(
        (mixed[:, -margin:, :], segment_ids[:, -margin:].astype(jnp.bfloat16)), "ctx", 1
    )
    mix_ext = jnp.concatenate([shifted_rows, mixed], axis=1).astype(jnp.float32)
    seg_ext = jnp.concatenate([shifted_segs.astype(jnp.int32), segment_ids], axis=1)

    def first_section(mix_in, weight_in, decay_in, rate_in):
        return jax.vmap(section_one, in_axes=(0, None, 0, 0, 0))(
            mix_in, weight_in, decay_in, rate_in, seg_ext
        )

    parts, first_pull = jax.vjp(first_section, mix_ext, conv_weight, log_decay, write_rate)
    transform, shift_term = jax.vmap(summarize)(parts)
    identity_pair = (
        jnp.broadcast_to(jnp.eye(transform.shape[-1], dtype=jnp.float32), transform.shape),
        jnp.zeros_like(shift_term),
    )
    incoming = prefix((transform, shift_term), "ctx", compose, identity_pair, False)[1]
    (outputs, leaving), second_pull = jax.vjp(jax.vmap(section_two), parts, incoming)
    part_grads, local_term = second_pull((cotangent.astype(jnp.float32), jnp.zeros_like(leaving)))
    flipped = jnp.swapaxes(transform, -1, -2)
    departing = prefix((flipped, local_term), "ctx", compose, identity_pair, True)[1]
    more_grads, unused_grad = second_pull((jnp.zeros_like(outputs), departing))
    total_parts = jax.tree.map(jnp.add, part_grads, more_grads)
    grad_mix, grad_weight, grad_decay, grad_rate = first_pull(total_parts)
    returned = from_behind(grad_mix[:, :margin, :].astype(jnp.bfloat16), "ctx", -1).astype(
        jnp.float32
    )
    own_grad = grad_mix[:, margin:, :]
    own_grad = jnp.concatenate(
        [own_grad[:, :-margin, :], own_grad[:, -margin:, :] + returned], axis=1
    )
    total_conv = lax.psum(grad_weight, ("dp", "ctx"))
    tokens_all = mixed.shape[0] * lax.axis_size("dp") * mixed.shape[1] * lax.axis_size("ctx")
    return (
        outputs.astype(jnp.bfloat16),
        own_grad.astype(jnp.bfloat16),
        grad_decay,
        grad_rate,
        total_conv / math.sqrt(tokens_all),
    )


def solution(mesh):
    in_specs = (
        P("dp", "ctx", None),
        P(),
        P("dp", "ctx", None),
        P("dp", "ctx", None),
        P("dp", "ctx"),
        P("dp", "ctx", None),
    )
    out_specs = (
        P("dp", "ctx", None),
        P("dp", "ctx", None),
        P("dp", "ctx", None),
        P("dp", "ctx", None),
        P(),
    )
    return jax.shard_map(local, mesh=mesh, in_specs=in_specs, out_specs=out_specs, check_vma=False)
```

profile of v0, /device:TPU:1, one launch (start us, length us, event | category | flops | bytes accessed | tf_op | source)
XLA Modules:
  0.0 655.9 jit_solution(14551815379886588994)
XLA Ops:
  9.2 4.5 collective-permute-start
  16.5 3.6 copy.804
  22.8 2.9 maximum_convert_fusion
  25.9 11.4 %fusion.293 = (f32[1,128,4096]{2,0,1:T(1,128)S(1)}, f32[1,128,4096]{2,0,1:T(1,128)}, f32[1,128,4096]{2,0,1:T(1,128)}) fusion(f32[1,131,4096]{2,0,1:T(1,128)S(1)} %maximum_convert_fusion, f32[4096]{0:T(1024)S(1)} %bitcast.948, f32[128]{0:T(128)S(1)} %get-tuple-element.1634, f32[4096]{0:T(1024)S(1)} %bitcast.950, f32[128]{0:T(128)S(1)} %get-tuple-element.1633, ...), kind=kLoop, calls=%fused_computation.432 | loop fusion | flops 7340032 | bytes 14747136 | tf_op jit(solution)/shard_map/jvp(vmap(jit(silu)))/mul | solution.py:51
  44.4 2.9 fusion.285
  74.4 14.4 %while.111 = (s32[]{:T(128)}, f32[1,16,128,128]{3,2,1,0:T(8,128)S(1)}, f32[1,16,128,128]{3,2,1,0:T(8,128)}, f32[2,1,16]{2,1,0:T(1,128)S(1)}, f32[2,1,16,64,128]{...) while((s32[]{:T(128)}, ...), condition=%wide.region_3.4_spmd, body=%wide.region_2.3_spmd.sunk | while | flops 1208778752 | bytes 22154000 | solution.py:182
  107.3 37.5 %all-gather.9.cloned.1.call-done = f32[8,16,128,128]{3,2,1,0:T(8,128)} async-done(((f32[1,16,128,128]{3,2,1,0:T(8,128)}), f32[8,16,128,128]{3,2,1,0:T(8,128)}) %all-gather.9.cloned.1.call-update) | async-done | bytes 8388624 | tf_op jit(solution)/shard_map/all_gather | solution.py:23
  144.8 56.7 %all-gather.11.cloned.1.call-done = f32[8,16,128,128]{3,2,1,0:T(8,128)} async-done(((f32[1,16,128,128]{3,2,1,0:T(8,128)}), f32[8,16,128,128]{3,2,1,0:T(8,128)}) %all-gather.11.cloned.1.call-update) | async-done | bytes 8388624 | tf_op jit(solution)/shard_map/all_gather | solution.py:23
  201.5 20.8 %while.114 = (s32[]{:T(128)}, f32[1,16,128,128]{3,2,1,0:T(8,128)S(1)}, s32[]{:T(128)}, f32[8,1,16,128,128]{4,3,2,1,0:T(8,128)}, f32[8,1,16,128,128]{4,3,2,1,0:T(8,128)}, /*index=5*/s32[]{:T(128)}, s32[]{:T(128)}) while((s32[]{:T(128)}, f32[1,16,128,128]{3,2,1,0:T(8,128)S(1)}, s32[]{:T(128)}, f32[8,1,16,128,128]{4,3,2,1,0:T(8,128)}, ...), condition=%wide.region_5.6_spmd.clone, body=%wide.region_4.5_spmd.clone.sunk | while | flops 403701760 | bytes 7342687 | solution.py:35
  201.6 2.8 fusion.468
  204.5 2.8 fusion.468
  207.5 2.8 fusion.468
  210.4 3.1 fusion.468
  213.6 2.8 fusion.468
  216.6 2.8 fusion.468
  219.5 2.8 fusion.468
  223.4 22.1 %while.112 = (s32[]{:T(128)}, f32[1,16,128,128]{3,2,1,0:T(8,128)S(1)}, bf16[2,1,16,64,128]{4,3,2,1,0:T(8,128)(2,1)}, f32[2,1,16,128,128]{3,4,2,1,0:T(8,128)S(1)}...) while((s32[]{:T(128)}, ...), condition=%wide.region_8.9_spmd, body=%wide.region_7.8_spmd.sunk | while | flops 705429504 | bytes 31461364 | solution.py:162
  223.4 3.2 bitcast_dynamic-update-slice_fusion.6
  230.9 3.6 fusion.442
  234.7 3.2 bitcast_dynamic-update-slice_fusion.6
  242.1 3.3 fusion.442
  251.1 33.2 %while.115 = (s32[]{:T(128)}, f32[1,16,128,128]{2,3,1,0:T(8,128)S(1)}, f32[2,1,16,64,128]{4,3,2,1,0:T(8,128)}, f32[2,1,16,64,128]{4,3,2,1,0:T(8,128)}, f32[2,1,1...) while((s32[]{:T(128)}, ...), condition=%wide.region_11.12_spmd.clone, body=%wide.region_9.11_spmd.clone.sunk | while | flops 1412038656 | bytes 66068172 | solution.py:162
  251.3 3.3 convolution_bitcast_fusion.42
  267.8 3.3 convolution_bitcast_fusion.42
  294.5 8.1 %reverse_bitcast_fusion.1 = f32[8,1,16,128,128]{4,3,2,1,0:T(8,128)} fusion(f32[8,16,128,128]{3,2,1,0:T(8,128)} %all-gather.13.cloned.1.call-done), kind=kLoop, calls=%fused_computation.184 | loop fusion | bytes 16777216
  302.6 37.5 %all-gather.15.cloned.1.call-done = f32[8,16,128,128]{3,2,1,0:T(8,128)} async-done(((f32[1,16,128,128]{3,2,1,0:T(8,128)}), f32[8,16,128,128]{3,2,1,0:T(8,128)}) %all-gather.15.cloned.1.call-update) | async-done | bytes 8388624 | tf_op jit(solution)/shard_map/all_gather | solution.py:23
  340.1 7.8 %reverse_bitcast_fusion = f32[8,1,16,128,128]{4,3,2,1,0:T(8,128)} fusion(f32[8,16,128,128]{3,2,1,0:T(8,128)} %all-gather.15.cloned.1.call-done), kind=kLoop, calls=%fused_computation.183 | loop fusion | bytes 16777216
  347.9 20.6 %while.116 = (s32[]{:T(128)}, f32[1,16,128,128]{3,2,1,0:T(8,128)S(1)}, s32[]{:T(128)}, f32[8,1,16,128,128]{4,3,2,1,0:T(8,128)}, f32[8,1,16,128,128]{4,3,2,1,0:T(8,128)}, /*index=5*/s32[]{:T(128)}, s32[]{:T(128)}) while((s32[]{:T(128)}, f32[1,16,128,128]{3,2,1,0:T(8,128)S(1)}, s32[]{:T(128)}, f32[8,1,16,128,128]{4,3,2,1,0:T(8,128)}, ...), condition=%wide.region_13.14_spmd.clone, body=%wide.region_12.13_spmd.clone.sunk | while | flops 403701760 | bytes 7342687 | solution.py:35
  348.0 2.8 fusion.489
  351.0 2.8 fusion.489
  353.9 2.8 fusion.489
  356.8 2.8 fusion.489
  359.8 2.8 fusion.489
  362.7 2.8 fusion.489
  365.6 2.9 fusion.489
  376.6 29.9 %while.113 = (s32[]{:T(128)}, f32[1,16,128,128]{2,3,1,0:T(8,128)S(1)}, f32[2,1,16,64,128]{4,3,2,1,0:T(8,128)}, f32[2,1,16,64,128]{4,3,2,1,0:T(8,128)}, f32[2,1,1...) while((s32[]{:T(128)}, ...), condition=%wide.region_16.17_spmd, body=%wide.region_14.16_spmd.sunk | while | flops 1410990080 | bytes 58727568 | solution.py:162
  376.6 3.3 convolution_bitcast_fusion.40
  391.5 3.3 convolution_bitcast_fusion.40
  443.1 5.6 fusion.187
  451.2 3.1 convolution_bitcast_fusion.17
  454.3 4.6 fusion.175
  475.6 4.7 fusion.160
  485.5 2.8 add_add_fusion.1
  488.4 16.1 %multiply_reduce_fusion.3 = (f32[4096]{0:T(1024)S(1)}, f32[4096]{0:T(1024)S(1)}, f32[4096]{0:T(1024)S(1)}, f32[4096]{0:T(1024)S(1)}, f32[1,128,4096]{2,0,1:T(1,128)S(1)}) fusion(f32[1,131,4096]{2,0,1:T(1,128)S(1)} %copy-done.3, f32[128]{0:T(128)S(1)} %copy-done.131, f32[128]{0:T(128)S(1)} %copy-done.129, f32[128]{0:T(128)S(1)} %copy-done.127, ...), kind=kLoop, calls=%fused_computation.199 | loop fusion | flops 9945088 | bytes 16844288 | tf_op jit(solution)/shard_map/transpose(jvp(vmap()))/reduce_sum | solution.py:47
  504.6 10.0 %broadcast_multiply_fusion = (f32[1,128,4096]{2,0,1:T(1,128)S(1)}, f32[1,128,4096]{2,0,1:T(1,128)S(1)}, f32[1,128,4096]{2,0,1:T(1,128)S(1)}, f32[1,128,4096]{2,0,1:T(1,128)S(1)}) fusion(f32[1,128,4096]{2,0,1:T(1,128)S(1)} %get-tuple-element.1584, f32[4096]{0:T(1024)S(1)} %bitcast.949, f32[128]{0:T(128)S(1)} %copy-done.127, f32[4096]{0:T(1024)S(1)} %bitcast.945, ...), kind=kLoop, calls=%fused_computation.292 | loop fusion | flops 3670016 | bytes 10552832 | tf_op jit(solution)/shard_map/transpose(jvp(vmap()))/mul | solution.py:47
  514.6 9.1 %fusion.290 = (bf16[1,131,4096]{2,0,1:T(2,128)(2,1)S(1)}, f32[1,131,4096]{2,0,1:T(1,128)}) fusion(f32[1,128,4096]{2,0,1:T(1,128)S(1)} %get-tuple-element.1602, f32[1,128,4096]{2,0,1:T(1,128)S(1)} %get-tuple-element.1603, f32[1,128,4096]{2,0,1:T(1,128)S(1)} %get-tuple-element.1604, f32[1,128,4096]{2,0,1:T(1,128)S(1)} %get-tuple-element.1601), kind=kLoop, calls=%fused_computation.430 | loop fusion | flops 2146304 | bytes 11608064 | tf_op jit(solution)/shard_map/convert.9
  537.1 2.8 pad_maximum_fusion
  542.0 105.6 %all-reduce.16.cloned.1.call-done = f32[4,4096]{1,0:T(4,128)} async-done(((f32[4,4096]{1,0:T(4,128)}), f32[4,4096]{1,0:T(4,128)}) %all-reduce.16.cloned.1.call-update) | async-done | bytes 65552 | tf_op jit(solution)/shard_map/psum | solution.py:229
  (593 shorter events, 234.3 us)
Async XLA Ops:
  7.2 13.4 %copy-start.134 = (s32[1,128]{1,0:T(1,128)S(1)}, s32[1,128]{1,0:T(1,128)}, u32[]{:S(2)}) copy-start(s32[1,128]{1,0:T(1,128)} %param.22) | copy-start | bytes 1540
  7.2 13.0 %copy-start.115 = (f32[4,4096]{1,0:T(4,128)S(1)}, f32[4,4096]{1,0:T(4,128)}, u32[]{:S(2)}) copy-start(f32[4,4096]{1,0:T(4,128)} %param.19) | copy-start | bytes 196612
  7.2 13.1 %copy-start.132 = (f32[1,128,16]{1,2,0:T(8,128)S(1)}, f32[1,128,16]{1,2,0:T(8,128)}, u32[]{:S(2)}) copy-start(f32[1,128,16]{1,2,0:T(8,128)} %param.20) | copy-start | bytes 24580
  7.2 13.5 %copy-start.133 = (f32[1,128,16]{1,2,0:T(8,128)S(1)}, f32[1,128,16]{1,2,0:T(8,128)}, u32[]{:S(2)}) copy-start(f32[1,128,16]{1,2,0:T(8,128)} %param.21) | copy-start | bytes 24580
  7.2 137.6 %all-gather.9.cloned.1.call-start = ((), (), s32[]{:S(2)}) async-start(), calls=%async_computation.1 | async-start | bytes 9437184 | tf_op jit(solution)/shard_map/all_gather | solution.py:23
  9.2 12.1 %collective-permute-start = (bf16[1,3]{1,0:T(2,128)(2,1)S(1)}, bf16[1,3]{1,0:T(2,128)(2,1)S(1)}, u32[]{:S(2)}, u32[]{:S(2)}) collective-permute-start(bf16[1,3]{1,0:T(2,128)(2,1)S(1)} %slice.83), channel_id=1, source_target_pairs={{0,1},{1,2},{2,3},{3,4},{4,5},{5,6},{6,7},{8,9},{9,10},{10,11},{11... | collective-permute-start | bytes 26 | tf_op jit(solution)/shard_map/ppermute | solution.py:18
  14.6 8.1 %collective-permute-start.1 = (bf16[1,3,4096]{2,1,0:T(4,128)(2,1)S(1)}, bf16[1,3,4096]{2,1,0:T(4,128)(2,1)S(1)}, u32[]{:S(2)}, u32[]{:S(2)}) collective-permute-start(bf16[1,3,4096]{2,1,0:T(4,128)(2,1)S(1)} %slice.87), channel_id=1, source_target_pairs={{0,1},{1,2},{2,3},{3,4},{4,5},{5,6},{6,7},{8,9},{9,10},{10,11},{11... | collective-permute-start | bytes 73736 | tf_op jit(solution)/shard_map/ppermute | solution.py:18
  20.3 5.5 copy-start.107
  20.3 5.5 copy-start.109
  20.3 5.5 copy-start.111
  20.3 5.5 copy-start.113
  20.5 5.2 copy-start.92
  20.5 5.2 copy-start.120
  20.8 5.0 copy-start.94
  20.9 37.8 %copy-start.97 = (f32[2,16,64]{2,1,0:T(8,128)}, f32[2,16,64]{2,1,0:T(8,128)S(1)}, u32[]{:S(2)}) copy-start(f32[2,16,64]{2,1,0:T(8,128)S(1)} %copy.813) | copy-start | bytes 24580
  21.2 47.7 %copy-start.101 = (f32[2,64,16]{1,2,0:T(8,128)}, f32[2,64,16]{1,2,0:T(8,128)S(1)}, u32[]{:S(2)}) copy-start(f32[2,64,16]{1,2,0:T(8,128)S(1)} %copy.834) | copy-start | bytes 24580
  21.3 37.4 %copy-start.99 = (pred[2,64,64]{1,2,0:T(8,128)(4,1)}, pred[2,64,64]{1,2,0:T(8,128)(4,1)S(1)}, u32[]{:S(2)}) copy-start(pred[2,64,64]{1,2,0:T(8,128)(4,1)S(1)} %get-tuple-element.1629) | copy-start | bytes 24580
  22.7 46.7 %copy-start.103 = (f32[2,64,16]{1,2,0:T(8,128)}, f32[2,64,16]{1,2,0:T(8,128)S(1)}, u32[]{:S(2)}) copy-start(f32[2,64,16]{1,2,0:T(8,128)S(1)} %copy.810) | copy-start | bytes 24580
  22.7 46.6 %copy-start.105 = (f32[2,64,16]{1,2,0:T(8,128)}, f32[2,64,16]{1,2,0:T(8,128)S(1)}, u32[]{:S(2)}) copy-start(f32[2,64,16]{1,2,0:T(8,128)S(1)} %copy.832) | copy-start | bytes 24580
  25.8 11.5 %copy-start.2 = (f32[1,131,4096]{2,0,1:T(1,128)}, f32[1,131,4096]{2,0,1:T(1,128)S(1)}, u32[]{:S(2)}) copy-start(f32[1,131,4096]{2,0,1:T(1,128)S(1)} %maximum_convert_fusion) | copy-start | bytes 6438916
  41.6 27.8 %copy-start.14 = (f32[128,8,2,128]{3,0,2,1:T(8,128)}, f32[128,8,2,128]{3,0,2,1:T(8,128)S(1)}, u32[]{:S(2)}) copy-start(f32[128,8,2,128]{3,0,2,1:T(8,128)S(1)} %broadcast_in_dim.262) | copy-start | bytes 3145732
  56.8 8.3 %copy-start.61 = (f32[2,16,64,64]{2,3,1,0:T(8,128)}, f32[2,16,64,64]{2,3,1,0:T(8,128)S(1)}, u32[]{:S(2)}) copy-start(f32[2,16,64,64]{2,3,1,0:T(8,128)S(1)} %copy.827) | copy-start | bytes 1572868
  58.7 8.3 %copy-start.45 = (f32[2,16,64,64]{2,3,1,0:T(8,128)}, f32[2,16,64,64]{2,3,1,0:T(8,128)S(1)}, u32[]{:S(2)}) copy-start(f32[2,16,64,64]{2,3,1,0:T(8,128)S(1)} %convolution_add_fusion.6) | copy-start | bytes 1572868
  61.0 4.1 copy-start.41
  62.9 4.1 copy-start.43
  88.8 4.3 copy-start.1
  88.8 4.3 copy-start.4
  89.8 111.7 %all-gather.11.cloned.1.call-start = ((), (), s32[]{:S(2)}) async-start(), calls=%async_computation.2 | async-start | bytes 9437184 | tf_op jit(solution)/shard_map/all_gather | solution.py:23
  90.5 204.0 %all-gather.13.cloned.1.call-start = ((), (), s32[]{:S(2)}) async-start(), calls=%async_computation.3 | async-start | bytes 9437184 | tf_op jit(solution)/shard_map/all_gather | solution.py:23
  93.2 246.9 %all-gather.15.cloned.1.call-start = ((), (), s32[]{:S(2)}) async-start(), calls=%async_computation.4 | async-start | bytes 9437184 | tf_op jit(solution)/shard_map/all_gather | solution.py:23
  223.4 4.2 copy-start.11
  223.4 4.2 copy-start.89
  234.6 4.2 copy-start.11
  234.6 4.2 copy-start.89
  246.7 4.4 copy-start
  285.7 362.0 %all-reduce.16.cloned.1.call-start = ((), (), s32[]{:S(2)}) async-start(), calls=%async_computation | async-start | bytes 131072 | tf_op jit(solution)/shard_map/psum | solution.py:229
  376.6 4.9 copy-start.6
  391.5 4.9 copy-start.6
  443.1 5.7 copy-start.16
  454.3 4.6 copy-start.32
  467.6 8.0 %copy-start.104 = (f32[2,64,16]{1,2,0:T(8,128)S(1)}, f32[2,64,16]{1,2,0:T(8,128)}, u32[]{:S(2)}) copy-start(f32[2,64,16]{1,2,0:T(8,128)} %copy-done.103) | copy-start | bytes 24580
  467.6 8.0 %copy-start.106 = (f32[2,64,16]{1,2,0:T(8,128)S(1)}, f32[2,64,16]{1,2,0:T(8,128)}, u32[]{:S(2)}) copy-start(f32[2,64,16]{1,2,0:T(8,128)} %copy-done.105) | copy-start | bytes 24580
  488.4 16.2 %copy-start.108 = (f32[1,4096]{1,0:T(1,128)S(1)}, f32[1,4096]{1,0:T(1,128)}, u32[]{:S(2)}) copy-start(f32[1,4096]{1,0:T(1,128)} %copy-done.107) | copy-start | bytes 49156
  488.4 16.2 %copy-start.110 = (f32[1,4096]{1,0:T(1,128)S(1)}, f32[1,4096]{1,0:T(1,128)}, u32[]{:S(2)}) copy-start(f32[1,4096]{1,0:T(1,128)} %copy-done.109) | copy-start | bytes 49156
  488.4 16.2 %copy-start.112 = (f32[1,4096]{1,0:T(1,128)S(1)}, f32[1,4096]{1,0:T(1,128)}, u32[]{:S(2)}) copy-start(f32[1,4096]{1,0:T(1,128)} %copy-done.111) | copy-start | bytes 49156
  488.4 16.2 %copy-start.114 = (f32[1,4096]{1,0:T(1,128)S(1)}, f32[1,4096]{1,0:T(1,128)}, u32[]{:S(2)}) copy-start(f32[1,4096]{1,0:T(1,128)} %copy-done.113) | copy-start | bytes 49156
  525.9 7.7 %copy-start.95 = (f32[1,128,16]{2,1,0:T(8,128)S(1)}, f32[1,128,16]{2,1,0:T(8,128)}, u32[]{:S(2)}) copy-start(f32[1,128,16]{2,1,0:T(8,128)} %copy-done.94) | copy-start | bytes 24580
  530.4 5.9 collective-permute-start.2
  (127 other events, 275.0 us)
Sparse Core Ops, SparseCore 0:
  89.9 54.8 all-gather.8
  147.2 54.2 all-gather.10
  203.4 54.2 all-gather.12
  285.8 54.2 all-gather.14
  526.8 120.8 all-reduce.15
where the time goes:
time: 666 us; the launch traced here: 656 us
  waiting for transfers between devices  238 us (36%)
  matrix products  200 us (30%)
  local copies, waits for them, and re-layouts  103 us (15%)
  other arithmetic  87.2 us (13%)
  between operations  16 us (2%)
  starting transfers between devices  9.43 us (1%)
    all_gather x4, waiting for transfers between devices, prefix(): pieces = jax.tree.map(lambda part: lax.all_gather(part, axis), value)  132 us
    psum x1, waiting for transfers between devices, local(): total_conv = lax.psum(grad_weight, ('dp', 'ctx'))  106 us
    dot_general x14, matrix products, compose(): jnp.einsum('shij,shjk->shik', later_map[0], earlier_map[1], precision=HIG...  39.8 us
    unnamed x227, local copies, waits for them, and re-layouts  33.5 us
    dot_general x15, matrix products, unit_lower_inverse(): jnp.einsum('hij,hjk->hik', result, identity_matrix + power, precision=HIG...  26.6 us
    dot_general x15, matrix products, unit_lower_inverse(): power = jnp.einsum('hij,hjk->hik', power, power, precision=HIGHEST)  25.9 us
    dot_general x10, matrix products, block_apply(): jnp.einsum('hcd,hce->hde', tail_keys, fresh_values, precision=HIGHEST)  24.3 us
    dot_general x10, matrix products, block_apply(): jnp.einsum('hcd,hde->hce', write_keys, state_in, precision=HIGHEST)  17.9 us
  transfers between devices with their start and end apart: 8, of which 4 were waited for; matrix products, arithmetic and copies ran while one was open for 20% of the time, Pallas kernels for 0%

commit v1 on v0

--- a/solution.py
+++ b/solution.py
@@ -226,7 +226,7 @@
     own_grad = jnp.concatenate(
         [own_grad[:, :-margin, :], own_grad[:, -margin:, :] + returned], axis=1
     )
-    total_conv = lax.psum(grad_weight, ("dp", "ctx"))
+    total_conv = jnp.sum(lax.all_gather(grad_weight, ("dp", "ctx")), axis=0)
     tokens_all = mixed.shape[0] * lax.axis_size("dp") * mixed.shape[1] * lax.axis_size("ctx")
     return (
         outputs.astype(jnp.bfloat16),

time: 666 us -> 581 us (0.87)
  waiting for transfers between devices: 238 us -> 156 us
    psum x1 -> x0, waiting for transfers between devices: 106 us -> none  [local(): total_conv = lax.psum(grad_weight, ('dp', 'ctx'))]
    all_gather x0 -> x1, waiting for transfers between devices: none -> 23.8 us  [local(): total_conv = jnp.sum(lax.all_gather(grad_weight, ('dp', 'ctx')), axis=0)]
  transfers between devices with their start and end apart: 8 -> 8, of which waited for: 4 -> 4; matrix products, arithmetic and copies ran while one was open for 20% -> 25% of each run, Pallas kernels for 0% -> 0%
where the time goes in v1:
time: 581 us; the launch traced here: 571 us
  matrix products  200 us (34%)
  waiting for transfers between devices  156 us (27%)
  local copies, waits for them, and re-layouts  102 us (18%)
  other arithmetic  85.5 us (15%)
  between operations  16.3 us (3%)
  starting transfers between devices  9.43 us (2%)
    all_gather x4, waiting for transfers between devices, prefix(): pieces = jax.tree.map(lambda part: lax.all_gather(part, axis), value)  132 us
    dot_general x14, matrix products, compose(): jnp.einsum('shij,shjk->shik', later_map[0], earlier_map[1], precision=HIG...  39.8 us
    unnamed x227, local copies, waits for them, and re-layouts  33.5 us
    dot_general x15, matrix products, unit_lower_inverse(): jnp.einsum('hij,hjk->hik', result, identity_matrix + power, precision=HIG...  26.6 us
    dot_general x15, matrix products, unit_lower_inverse(): power = jnp.einsum('hij,hjk->hik', power, power, precision=HIGHEST)  25.4 us
    dot_general x10, matrix products, block_apply(): jnp.einsum('hcd,hce->hde', tail_keys, fresh_values, precision=HIGHEST)  24.3 us
    all_gather x1, waiting for transfers between devices, local(): total_conv = jnp.sum(lax.all_gather(grad_weight, ('dp', 'ctx')), axis=0)  23.8 us
    dot_general x10, matrix products, block_apply(): jnp.einsum('hcd,hde->hce', write_keys, state_in, precision=HIGHEST)  17.9 us
  transfers between devices with their start and end apart: 8, of which 4 were waited for; matrix products, arithmetic and copies ran while one was open for 25% of the time, Pallas kernels for 0%

profile of v1, /device:TPU:1, one launch (start us, length us, event | category | flops | bytes accessed | tf_op | source)
XLA Modules:
  0.0 570.7 jit_solution(2825754224643326568)
XLA Ops:
  9.2 4.5 collective-permute-start
  16.5 3.6 copy.804
  22.8 2.9 maximum_convert_fusion
  25.9 11.4 %fusion.293 = (f32[1,128,4096]{2,0,1:T(1,128)S(1)}, f32[1,128,4096]{2,0,1:T(1,128)}, f32[1,128,4096]{2,0,1:T(1,128)}) fusion(f32[1,131,4096]{2,0,1:T(1,128)S(1)} %maximum_convert_fusion, f32[4096]{0:T(1024)S(1)} %bitcast.950, f32[128]{0:T(128)S(1)} %get-tuple-element.1634, f32[4096]{0:T(1024)S(1)} %bitcast.952, f32[128]{0:T(128)S(1)} %get-tuple-element.1633, ...), kind=kLoop, calls=%fused_computation.432 | loop fusion | flops 7340032 | bytes 14747136 | tf_op jit(solution)/shard_map/jvp(vmap(jit(silu)))/mul | solution.py:51
  44.4 2.9 fusion.285
  74.5 14.4 %while.111 = (s32[]{:T(128)}, f32[1,16,128,128]{3,2,1,0:T(8,128)S(1)}, f32[1,16,128,128]{3,2,1,0:T(8,128)}, f32[2,1,16]{2,1,0:T(1,128)S(1)}, f32[2,1,16,64,128]{...) while((s32[]{:T(128)}, ...), condition=%wide.region_3.4_spmd, body=%wide.region_2.3_spmd.sunk | while | flops 1208778752 | bytes 22154000 | solution.py:182
  107.4 37.5 %all-gather.12.cloned.1.call-done = f32[8,16,128,128]{3,2,1,0:T(8,128)} async-done(((f32[1,16,128,128]{3,2,1,0:T(8,128)}), f32[8,16,128,128]{3,2,1,0:T(8,128)}) %all-gather.12.cloned.1.call-update) | async-done | bytes 8388624 | tf_op jit(solution)/shard_map/all_gather | solution.py:23
  144.8 56.7 %all-gather.14.cloned.1.call-done = f32[8,16,128,128]{3,2,1,0:T(8,128)} async-done(((f32[1,16,128,128]{3,2,1,0:T(8,128)}), f32[8,16,128,128]{3,2,1,0:T(8,128)}) %all-gather.14.cloned.1.call-update) | async-done | bytes 8388624 | tf_op jit(solution)/shard_map/all_gather | solution.py:23
  201.6 20.8 %while.114 = (s32[]{:T(128)}, f32[1,16,128,128]{3,2,1,0:T(8,128)S(1)}, s32[]{:T(128)}, f32[8,1,16,128,128]{4,3,2,1,0:T(8,128)}, f32[8,1,16,128,128]{4,3,2,1,0:T(8,128)}, /*index=5*/s32[]{:T(128)}, s32[]{:T(128)}) while((s32[]{:T(128)}, f32[1,16,128,128]{3,2,1,0:T(8,128)S(1)}, s32[]{:T(128)}, f32[8,1,16,128,128]{4,3,2,1,0:T(8,128)}, ...), condition=%wide.region_5.6_spmd.clone, body=%wide.region_4.5_spmd.clone.sunk | while | flops 403701760 | bytes 7342687 | solution.py:35
  201.7 2.8 fusion.468
  204.6 2.8 fusion.468
  207.5 2.8 fusion.468
  210.5 3.1 fusion.468
  213.7 2.8 fusion.468
  216.6 2.8 fusion.468
  219.6 2.8 fusion.468
  223.5 22.1 %while.112 = (s32[]{:T(128)}, f32[1,16,128,128]{3,2,1,0:T(8,128)S(1)}, bf16[2,1,16,64,128]{4,3,2,1,0:T(8,128)(2,1)}, f32[2,1,16,128,128]{3,4,2,1,0:T(8,128)S(1)}...) while((s32[]{:T(128)}, ...), condition=%wide.region_8.9_spmd, body=%wide.region_7.8_spmd.sunk | while | flops 705429504 | bytes 31461364 | solution.py:162
  223.5 3.2 bitcast_dynamic-update-slice_fusion.6
  230.9 3.6 fusion.442
  234.7 3.2 bitcast_dynamic-update-slice_fusion.6
  242.2 3.3 fusion.442
  251.2 33.2 %while.115 = (s32[]{:T(128)}, f32[1,16,128,128]{2,3,1,0:T(8,128)S(1)}, f32[2,1,16,64,128]{4,3,2,1,0:T(8,128)}, f32[2,1,16,64,128]{4,3,2,1,0:T(8,128)}, f32[2,1,1...) while((s32[]{:T(128)}, ...), condition=%wide.region_11.12_spmd.clone, body=%wide.region_9.11_spmd.clone.sunk | while | flops 1412038656 | bytes 66068172 | solution.py:162
  251.4 3.3 convolution_bitcast_fusion.42
  267.9 3.3 convolution_bitcast_fusion.42
  294.5 8.1 %reverse_bitcast_fusion.1 = f32[8,1,16,128,128]{4,3,2,1,0:T(8,128)} fusion(f32[8,16,128,128]{3,2,1,0:T(8,128)} %all-gather.16.cloned.1.call-done), kind=kLoop, calls=%fused_computation.184 | loop fusion | bytes 16777216
  302.6 37.5 %all-gather.18.cloned.1.call-done = f32[8,16,128,128]{3,2,1,0:T(8,128)} async-done(((f32[1,16,128,128]{3,2,1,0:T(8,128)}), f32[8,16,128,128]{3,2,1,0:T(8,128)}) %all-gather.18.cloned.1.call-update) | async-done | bytes 8388624 | tf_op jit(solution)/shard_map/all_gather | solution.py:23
  340.2 7.8 %reverse_bitcast_fusion = f32[8,1,16,128,128]{4,3,2,1,0:T(8,128)} fusion(f32[8,16,128,128]{3,2,1,0:T(8,128)} %all-gather.18.cloned.1.call-done), kind=kLoop, calls=%fused_computation.183 | loop fusion | bytes 16777216
  348.0 20.6 %while.116 = (s32[]{:T(128)}, f32[1,16,128,128]{3,2,1,0:T(8,128)S(1)}, s32[]{:T(128)}, f32[8,1,16,128,128]{4,3,2,1,0:T(8,128)}, f32[8,1,16,128,128]{4,3,2,1,0:T(8,128)}, /*index=5*/s32[]{:T(128)}, s32[]{:T(128)}) while((s32[]{:T(128)}, f32[1,16,128,128]{3,2,1,0:T(8,128)S(1)}, s32[]{:T(128)}, f32[8,1,16,128,128]{4,3,2,1,0:T(8,128)}, ...), condition=%wide.region_13.14_spmd.clone, body=%wide.region_12.13_spmd.clone.sunk | while | flops 403701760 | bytes 7342687 | solution.py:35
  348.1 2.8 fusion.489
  351.0 2.8 fusion.489
  353.9 2.8 fusion.489
  356.9 2.8 fusion.489
  359.8 2.8 fusion.489
  362.8 2.8 fusion.489
  365.7 2.9 fusion.489
  376.7 29.9 %while.113 = (s32[]{:T(128)}, f32[1,16,128,128]{2,3,1,0:T(8,128)S(1)}, f32[2,1,16,64,128]{4,3,2,1,0:T(8,128)}, f32[2,1,16,64,128]{4,3,2,1,0:T(8,128)}, f32[2,1,1...) while((s32[]{:T(128)}, ...), condition=%wide.region_16.17_spmd, body=%wide.region_14.16_spmd.sunk | while | flops 1410990080 | bytes 58727568 | solution.py:162
  376.7 3.3 convolution_bitcast_fusion.40
  391.5 3.3 convolution_bitcast_fusion.40
  443.2 5.1 fusion.187
  450.7 3.1 convolution_bitcast_fusion.17
  453.8 4.6 fusion.175
  475.1 4.7 fusion.160
  485.0 2.8 add_add_fusion.1
  487.9 16.2 %multiply_reduce_fusion.3 = (f32[4096]{0:T(1024)S(1)}, f32[4096]{0:T(1024)S(1)}, f32[4096]{0:T(1024)S(1)}, f32[4096]{0:T(1024)S(1)}, f32[1,128,4096]{2,0,1:T(1,128)S(1)}) fusion(f32[1,131,4096]{2,0,1:T(1,128)S(1)} %copy-done.3, f32[128]{0:T(128)S(1)} %copy-done.132, f32[128]{0:T(128)S(1)} %copy-done.130, f32[128]{0:T(128)S(1)} %copy-done.128, ...), kind=kLoop, calls=%fused_computation.199 | loop fusion | flops 9945088 | bytes 16844288 | tf_op jit(solution)/shard_map/transpose(jvp(vmap()))/reduce_sum | solution.py:47
  505.8 9.7 %broadcast_multiply_fusion = (f32[1,128,4096]{2,0,1:T(1,128)S(1)}, f32[1,128,4096]{2,0,1:T(1,128)S(1)}, f32[1,128,4096]{2,0,1:T(1,128)S(1)}, f32[1,128,4096]{2,0,1:T(1,128)S(1)}) fusion(f32[1,128,4096]{2,0,1:T(1,128)S(1)} %get-tuple-element.1584, f32[4096]{0:T(1024)S(1)} %bitcast.951, f32[128]{0:T(128)S(1)} %copy-done.128, f32[4096]{0:T(1024)S(1)} %bitcast.947, ...), kind=kLoop, calls=%fused_computation.292 | loop fusion | flops 3670016 | bytes 10552832 | tf_op jit(solution)/shard_map/transpose(jvp(vmap()))/mul | solution.py:47
  515.6 9.1 %fusion.290 = (bf16[1,131,4096]{2,0,1:T(2,128)(2,1)S(1)}, f32[1,131,4096]{2,0,1:T(1,128)}) fusion(f32[1,128,4096]{2,0,1:T(1,128)S(1)} %get-tuple-element.1602, f32[1,128,4096]{2,0,1:T(1,128)S(1)} %get-tuple-element.1603, f32[1,128,4096]{2,0,1:T(1,128)S(1)} %get-tuple-element.1604, f32[1,128,4096]{2,0,1:T(1,128)S(1)} %get-tuple-element.1601), kind=kLoop, calls=%fused_computation.430 | loop fusion | flops 2146304 | bytes 11608064 | tf_op jit(solution)/shard_map/convert.9
  532.5 2.8 pad_maximum_fusion
  537.4 23.8 %all-gather.20.cloned.1.call-done = f32[32,4,4096]{2,1,0:T(4,128)} async-done(((f32[1,4,4096]{2,1,0:T(4,128)}), f32[32,4,4096]{2,1,0:T(4,128)}) %all-gather.20.cloned.1.call-update) | async-done | bytes 2097168 | tf_op jit(solution)/shard_map/all_gather | solution.py:229
  (594 shorter events, 231.5 us)
Async XLA Ops:
  7.2 13.4 %copy-start.135 = (s32[1,128]{1,0:T(1,128)S(1)}, s32[1,128]{1,0:T(1,128)}, u32[]{:S(2)}) copy-start(s32[1,128]{1,0:T(1,128)} %param.22) | copy-start | bytes 1540
  7.2 13.0 %copy-start.115 = (f32[4,4096]{1,0:T(4,128)S(1)}, f32[4,4096]{1,0:T(4,128)}, u32[]{:S(2)}) copy-start(f32[4,4096]{1,0:T(4,128)} %param.19) | copy-start | bytes 196612
  7.2 13.1 %copy-start.133 = (f32[1,128,16]{1,2,0:T(8,128)S(1)}, f32[1,128,16]{1,2,0:T(8,128)}, u32[]{:S(2)}) copy-start(f32[1,128,16]{1,2,0:T(8,128)} %param.20) | copy-start | bytes 24580
  7.2 13.5 %copy-start.134 = (f32[1,128,16]{1,2,0:T(8,128)S(1)}, f32[1,128,16]{1,2,0:T(8,128)}, u32[]{:S(2)}) copy-start(f32[1,128,16]{1,2,0:T(8,128)} %param.21) | copy-start | bytes 24580
  7.2 137.6 %all-gather.12.cloned.1.call-start = ((), (), s32[]{:S(2)}) async-start(), calls=%async_computation | async-start | bytes 9437184 | tf_op jit(solution)/shard_map/all_gather | solution.py:23
  9.2 12.1 %collective-permute-start = (bf16[1,3]{1,0:T(2,128)(2,1)S(1)}, bf16[1,3]{1,0:T(2,128)(2,1)S(1)}, u32[]{:S(2)}, u32[]{:S(2)}) collective-permute-start(bf16[1,3]{1,0:T(2,128)(2,1)S(1)} %slice.83), channel_id=1, source_target_pairs={{0,1},{1,2},{2,3},{3,4},{4,5},{5,6},{6,7},{8,9},{9,10},{10,11},{11... | collective-permute-start | bytes 26 | tf_op jit(solution)/shard_map/ppermute | solution.py:18
  14.6 8.2 %collective-permute-start.1 = (bf16[1,3,4096]{2,1,0:T(4,128)(2,1)S(1)}, bf16[1,3,4096]{2,1,0:T(4,128)(2,1)S(1)}, u32[]{:S(2)}, u32[]{:S(2)}) collective-permute-start(bf16[1,3,4096]{2,1,0:T(4,128)(2,1)S(1)} %slice.87), channel_id=1, source_target_pairs={{0,1},{1,2},{2,3},{3,4},{4,5},{5,6},{6,7},{8,9},{9,10},{10,11},{11... | collective-permute-start | bytes 73736 | tf_op jit(solution)/shard_map/ppermute | solution.py:18
  20.3 5.6 copy-start.107
  20.3 5.6 copy-start.109
  20.3 5.6 copy-start.111
  20.3 5.6 copy-start.113
  20.5 5.3 copy-start.92
  20.5 5.3 copy-start.120
  20.8 5.0 copy-start.94
  20.9 37.9 %copy-start.97 = (f32[2,16,64]{2,1,0:T(8,128)}, f32[2,16,64]{2,1,0:T(8,128)S(1)}, u32[]{:S(2)}) copy-start(f32[2,16,64]{2,1,0:T(8,128)S(1)} %copy.813) | copy-start | bytes 24580
  21.2 47.7 %copy-start.101 = (f32[2,64,16]{1,2,0:T(8,128)}, f32[2,64,16]{1,2,0:T(8,128)S(1)}, u32[]{:S(2)}) copy-start(f32[2,64,16]{1,2,0:T(8,128)S(1)} %copy.834) | copy-start | bytes 24580
  21.3 37.5 %copy-start.99 = (pred[2,64,64]{1,2,0:T(8,128)(4,1)}, pred[2,64,64]{1,2,0:T(8,128)(4,1)S(1)}, u32[]{:S(2)}) copy-start(pred[2,64,64]{1,2,0:T(8,128)(4,1)S(1)} %get-tuple-element.1629) | copy-start | bytes 24580
  22.7 46.7 %copy-start.103 = (f32[2,64,16]{1,2,0:T(8,128)}, f32[2,64,16]{1,2,0:T(8,128)S(1)}, u32[]{:S(2)}) copy-start(f32[2,64,16]{1,2,0:T(8,128)S(1)} %copy.810) | copy-start | bytes 24580
  22.8 46.6 %copy-start.105 = (f32[2,64,16]{1,2,0:T(8,128)}, f32[2,64,16]{1,2,0:T(8,128)S(1)}, u32[]{:S(2)}) copy-start(f32[2,64,16]{1,2,0:T(8,128)S(1)} %copy.832) | copy-start | bytes 24580
  25.8 11.5 %copy-start.2 = (f32[1,131,4096]{2,0,1:T(1,128)}, f32[1,131,4096]{2,0,1:T(1,128)S(1)}, u32[]{:S(2)}) copy-start(f32[1,131,4096]{2,0,1:T(1,128)S(1)} %maximum_convert_fusion) | copy-start | bytes 6438916
  41.6 27.8 %copy-start.14 = (f32[128,8,2,128]{3,0,2,1:T(8,128)}, f32[128,8,2,128]{3,0,2,1:T(8,128)S(1)}, u32[]{:S(2)}) copy-start(f32[128,8,2,128]{3,0,2,1:T(8,128)S(1)} %broadcast_in_dim.262) | copy-start | bytes 3145732
  56.9 8.3 %copy-start.61 = (f32[2,16,64,64]{2,3,1,0:T(8,128)}, f32[2,16,64,64]{2,3,1,0:T(8,128)S(1)}, u32[]{:S(2)}) copy-start(f32[2,16,64,64]{2,3,1,0:T(8,128)S(1)} %copy.827) | copy-start | bytes 1572868
  58.8 8.3 %copy-start.45 = (f32[2,16,64,64]{2,3,1,0:T(8,128)}, f32[2,16,64,64]{2,3,1,0:T(8,128)S(1)}, u32[]{:S(2)}) copy-start(f32[2,16,64,64]{2,3,1,0:T(8,128)S(1)} %convolution_add_fusion.6) | copy-start | bytes 1572868
  88.9 4.3 copy-start.1
  88.9 4.3 copy-start.4
  89.8 111.7 %all-gather.14.cloned.1.call-start = ((), (), s32[]{:S(2)}) async-start(), calls=%async_computation.1 | async-start | bytes 9437184 | tf_op jit(solution)/shard_map/all_gather | solution.py:23
  90.6 203.9 %all-gather.16.cloned.1.call-start = ((), (), s32[]{:S(2)}) async-start(), calls=%async_computation.2 | async-start | bytes 9437184 | tf_op jit(solution)/shard_map/all_gather | solution.py:23
  93.2 247.0 %all-gather.18.cloned.1.call-start = ((), (), s32[]{:S(2)}) async-start(), calls=%async_computation.3 | async-start | bytes 9437184 | tf_op jit(solution)/shard_map/all_gather | solution.py:23
  246.7 4.4 copy-start
  285.7 275.5 %all-gather.20.cloned.1.call-start = ((), (), s32[]{:S(2)}) async-start(), calls=%async_computation.4 | async-start | bytes 2162688 | tf_op jit(solution)/shard_map/all_gather | solution.py:229
  376.7 4.9 copy-start.6
  391.5 4.9 copy-start.6
  443.2 5.1 copy-start.16
  453.8 4.6 copy-start.32
  467.1 8.0 %copy-start.104 = (f32[2,64,16]{1,2,0:T(8,128)S(1)}, f32[2,64,16]{1,2,0:T(8,128)}, u32[]{:S(2)}) copy-start(f32[2,64,16]{1,2,0:T(8,128)} %copy-done.103) | copy-start | bytes 24580
  467.1 8.0 %copy-start.106 = (f32[2,64,16]{1,2,0:T(8,128)S(1)}, f32[2,64,16]{1,2,0:T(8,128)}, u32[]{:S(2)}) copy-start(f32[2,64,16]{1,2,0:T(8,128)} %copy-done.105) | copy-start | bytes 24580
  487.9 17.3 %copy-start.96 = (f32[1,2,16,64,64]{3,4,2,1,0:T(8,128)S(1)}, f32[1,2,16,64,64]{3,4,2,1,0:T(8,128)}, u32[]{:S(2)}) copy-start(f32[1,2,16,64,64]{3,4,2,1,0:T(8,128)} %get-tuple-element.1599) | copy-start | bytes 1572868
  487.9 17.9 %copy-start.108 = (f32[1,4096]{1,0:T(1,128)S(1)}, f32[1,4096]{1,0:T(1,128)}, u32[]{:S(2)}) copy-start(f32[1,4096]{1,0:T(1,128)} %copy-done.107) | copy-start | bytes 49156
  487.9 17.9 %copy-start.110 = (f32[1,4096]{1,0:T(1,128)S(1)}, f32[1,4096]{1,0:T(1,128)}, u32[]{:S(2)}) copy-start(f32[1,4096]{1,0:T(1,128)} %copy-done.109) | copy-start | bytes 49156
  487.9 17.9 %copy-start.112 = (f32[1,4096]{1,0:T(1,128)S(1)}, f32[1,4096]{1,0:T(1,128)}, u32[]{:S(2)}) copy-start(f32[1,4096]{1,0:T(1,128)} %copy-done.111) | copy-start | bytes 49156
  487.9 17.9 %copy-start.114 = (f32[1,4096]{1,0:T(1,128)S(1)}, f32[1,4096]{1,0:T(1,128)}, u32[]{:S(2)}) copy-start(f32[1,4096]{1,0:T(1,128)} %copy-done.113) | copy-start | bytes 49156
  515.5 11.7 %copy-start.93 = (f32[1,2,64,16]{3,2,1,0:T(8,128)S(1)}, f32[1,2,64,16]{3,2,1,0:T(8,128)}, u32[]{:S(2)}) copy-start(f32[1,2,64,16]{3,2,1,0:T(8,128)} %copy-done.92) | copy-start | bytes 24580
  515.5 11.7 %copy-start.121 = (f32[1,2,1,16]{3,2,1,0:T(1,128)S(1)}, f32[1,2,1,16]{3,2,1,0:T(1,128)}, u32[]{:S(2)}) copy-start(f32[1,2,1,16]{3,2,1,0:T(1,128)} %copy-done.120) | copy-start | bytes 388
  515.5 11.7 %copy-start.123 = (f32[2,64]{1,0:T(2,128)S(1)}, f32[2,64]{1,0:T(2,128)}, u32[]{:S(2)}) copy-start(f32[2,64]{1,0:T(2,128)} %copy-done.122) | copy-start | bytes 1540
  515.5 11.8 %copy-start.137 = (f32[2]{0:T(128)S(1)}, f32[2]{0:T(128)}, u32[]{:S(2)}) copy-start(f32[2]{0:T(128)} %copy-done.136) | copy-start | bytes 28
  515.5 11.9 %copy-start.95 = (f32[1,128,16]{2,1,0:T(8,128)S(1)}, f32[1,128,16]{2,1,0:T(8,128)}, u32[]{:S(2)}) copy-start(f32[1,128,16]{2,1,0:T(8,128)} %copy-done.94) | copy-start | bytes 24580
  515.6 11.9 %copy-start.126 = (f32[2,64]{1,0:T(2,128)S(1)}, f32[2,64]{1,0:T(2,128)}, u32[]{:S(2)}) copy-start(f32[2,64]{1,0:T(2,128)} %copy-done.125) | copy-start | bytes 1540
  524.8 6.8 %collective-permute-start.2 = (bf16[1,3,4096]{2,1,0:T(4,128)(2,1)S(1)}, bf16[1,3,4096]{2,1,0:T(4,128)(2,1)S(1)}, u32[]{:S(2)}, u32[]{:S(2)}) collective-permute-start(bf16[1,3,4096]{2,1,0:T(4,128)(2,1)S(1)} %copy.926), channel_id=1, source_target_pairs={{1,0},{2,1},{3,2},{4,3},{5,4},{6,5},{7,6},{9,8},{10,9},{11,10},{12... | collective-permute-start | bytes 73736 | tf_op jit(solution)/shard_map/ppermute | solution.py:18
  (127 other events, 281.2 us)
Sparse Core Ops, SparseCore 0:
  90.0 54.8 all-gather.11
  147.3 54.2 all-gather.13
  203.5 54.2 all-gather.15
  285.8 54.3 all-gather.17
  505.0 56.1 all-gather.19
